TPU v7x, 256 devices: a whole 4x4x8 slice. The times are simulated.
256 devices in a mesh: space: 64 (over y, z, core), pa: 2 (over x_lo), pb: 2 (over x_hi).
Axes of the slice: x: 4 (x_hi: 2, x_lo: 2; x = x_hi * 2 + x_lo), y: 4, z: 8, core: 2. Of those that a mesh axis runs over, the one named last changes fastest.
Arguments:
- field: float32 [8192, 16, 16, 16, 16], P('space', 'pa', None, 'pb'), may hold values from -6 to 6
- g_first: float32 [16, 128], P('pa'), may hold values from -1.5 to 1.5
- g_second: float32 [16, 128], replicated, may hold values from -1.5 to 1.5
- g_third: float32 [16, 128], P('pb'), may hold values from -1.5 to 1.5
- g_fourth: float32 [16, 128], replicated, may hold values from -1.5 to 1.5
- h_second: float32 [16, 128], replicated, may hold values from -1.5 to 1.5
- h_third: float32 [16, 128], P('pb'), may hold values from -1.5 to 1.5
- h_fourth: float32 [16, 128], replicated, may hold values from -1.5 to 1.5
Outputs:
- basis: float32 [8192, 128], P('space')
- core: float32 [128, 16, 16, 16, 16], P('space', 'pa', None, 'pb')
- next_sketch: float32 [128, 16, 128], P('space', 'pa')
All inputs are finite; a program needn't handle non-finite values.
Results may differ from a plain program's by a relative error of at most 0.00011.
Values sent between devices are 32-bit elements; how exact they have to be, the bound alone decides.
No kernel may reach another device: no remote copies, remote signals or barrier semaphores. Data moves between devices by JAX's collectives and lax.ppermute only.
A program may use at most 128 MiB of HBM per device.

v0:
```python
import jax
import jax.numpy as jnp
from jax import lax
from jax.sharding import PartitionSpec as P

MODE = 16
RANK = 128


def body(field, g_first, g_second, g_third, g_fourth, h_second, h_third, h_fourth):
    highest = lax.Precision.HIGHEST
    rows = field.shape[0]
    first_loc = field.shape[1]
    third_loc = field.shape[3]
    width = first_loc * MODE * third_loc * MODE
    flat = field.reshape(rows, width)
    omega = (
        g_first[:, None, None, None, :]
        * g_second[None, :, None, None, :]
        * g_third[None, None, :, None, :]
        * g_fourth[None, None, None, :, :]
    ).reshape(width, RANK)
    partial_sketch = jnp.dot(flat, omega, precision=highest, preferred_element_type=jnp.float32)
    sketch = lax.psum(partial_sketch, ("pa", "pb"))
    gram = lax.psum(
        jnp.dot(sketch.T, sketch, precision=highest, preferred_element_type=jnp.float32), "space"
    )
    lower = jnp.linalg.cholesky(gram)
    basis = lax.linalg.triangular_solve(
        lower, sketch, left_side=False, lower=True, transpose_a=True
    )
    core_flat = lax.psum_scatter(
        lax.dot_general(
            basis,
            flat,
            (((0,), (0,)), ((), ())),
            precision=highest,
            preferred_element_type=jnp.float32,
        ),
        "space",
        scatter_dimension=0,
        tiled=True,
    )
    own_rank = core_flat.shape[0]
    psi = (
        h_second[:, None, None, :] * h_third[None, :, None, :] * h_fourth[None, None, :, :]
    ).reshape(MODE * third_loc * MODE, RANK)
    partial_next = jnp.dot(
        core_flat.reshape(own_rank * first_loc, MODE * third_loc * MODE),
        psi,
        precision=highest,
        preferred_element_type=jnp.float32,
    )
    next_sketch = lax.psum(partial_next, "pb")
    core = core_flat.reshape(own_rank, first_loc, MODE, third_loc, MODE)
    return (basis, core, next_sketch.reshape(own_rank, first_loc, RANK))


def solution(mesh):
    placed = (
        P("space", "pa", None, "pb", None),
        P("pa", None),
        P(),
        P("pb", None),
        P(),
        P(),
        P("pb", None),
        P(),
    )
    return jax.shard_map(
        body,
        mesh=mesh,
        in_specs=placed,
        out_specs=(P("space", None), P("space", "pa", None, "pb", None), P("space", "pa", None)),
        check_vma=False,
    )
```

profile of v0, /device:TPU:2, one launch (start us, length us, event | category | flops | bytes accessed | tf_op | source)
XLA Modules:
  0.0 507.3 jit_solution(7857300615730254369)
XLA Ops:
  7.2 0.0 all-reduce.5.cloned.1.call-start
  7.2 0.7 broadcast_multiply_fusion.3
  7.9 0.7 broadcast_multiply_fusion.1
  8.6 16.7 %fusion.4 = f32[128,128]{0,1:T(8,128)} fusion(f32[128,8,16,8,16]{0,4,3,2,1:T(8,128)} %param.8, f32[16,128]{1,0:T(8,128)} %param.12, f32[8,16,8,128]{3,2,1,0:T(8,128)S(1)} %broadcast_multiply_fusion.1), kind=kOutput, calls=%fused_computation.4 | convolution fusion | flops 3223322624 | bytes 8986624 | tf_op jit(solution)/shard_map/dot_general | solution.py:23
  25.4 0.0 all-reduce.5.cloned.1.call-update
  25.4 0.0 all-reduce.7.cloned.1.call-start
  25.4 48.2 %all-reduce.5.cloned.1.call-done = f32[128,128]{0,1:T(8,128)} async-done(((f32[128,128]{0,1:T(8,128)}), f32[128,128]{0,1:T(8,128)}) %all-reduce.5.cloned.1.call-update) | async-done | bytes 65552 | tf_op jit(solution)/shard_map/psum | solution.py:24
  73.6 1.8 fusion.11
  75.4 0.0 all-reduce.7.cloned.1.call-update
  75.4 0.2 all-reduce.9.cloned.1.call-start
  75.6 174.4 %all-reduce.7.cloned.1.call-done = f32[128,128]{0,1:T(8,128)} async-done(((f32[128,128]{0,1:T(8,128)}), f32[128,128]{0,1:T(8,128)}) %all-reduce.7.cloned.1.call-update) | async-done | bytes 65552 | tf_op jit(solution)/shard_map/psum | solution.py:25
  250.1 0.9 copy.14
  251.0 0.9 fusion.10
  251.9 11.7 %cholesky.16 = f32[128,128]{1,0:T(8,128)S(1)} custom-call(f32[128,128]{1,0:T(8,128)S(1)} %fusion.10), custom_call_target="Cholesky" | custom-call | tf_op jit(solution)/shard_map/jit(cholesky)/cholesky | solution.py:28
  263.6 0.6 compare_reduce_fusion
  264.2 0.7 fusion.7
  264.9 9.8 %custom-call.6 = f32[1,128,128]{1,2,0:T(8,128)S(1)} custom-call(f32[1,128,128]{2,1,0:T(8,128)S(1)} %fusion.7), custom_call_target="InvertDiagBlocksLowerTriangular" | custom-call | tf_op jit(solution)/shard_map/triangular_solve | solution.py:29
  274.7 1.1 fusion.8
  275.9 0.0 copy-start
  275.9 12.1 %fusion.12 = f32[128,16384]{1,0:T(8,128)} fusion(f32[128,128]{1,0:T(8,128)S(1)} %fusion.8, f32[128,16384]{0,1:T(8,128)} %bitcast.28), kind=kOutput, calls=%fused_computation.22 | convolution fusion | flops 3221225472 | bytes 16842752 | tf_op jit(solution)/shard_map/dot_general | solution.py:33
  287.9 0.0 copy-start.3
  287.9 0.0 copy-start.1
  288.0 0.0 all-reduce.9.cloned.1.call-update
  288.0 0.6 copy-done.4
  288.6 0.6 dynamic-slice
  289.9 0.1 broadcast_multiply_fusion
  290.0 200.5 %all-reduce.9.cloned.1.call-done = f32[128,16384]{1,0:T(8,128)} async-done(((f32[128,16384]{1,0:T(8,128)}), f32[128,16384]{1,0:T(8,128)}) %all-reduce.9.cloned.1.call-update) | async-done | bytes 8388624
  490.5 1.1 constant_dynamic-slice_fusion
  491.6 0.1 reshape.68
  491.7 1.4 reshape.67
  493.1 0.6 convolution_bitcast_fusion
  493.7 7.1 %psum.23 = f32[2,8,128]{2,1,0:T(8,128)} all-reduce(f32[2,8,128]{2,1,0:T(8,128)S(1)} %convolution_bitcast_fusion), channel_id=1, replica_groups=mesh['space'=64,'pa'=2,'pb'=2] {'pb'}, use_global_device_ids=true, to_apply=%region_5.6 | all-reduce | flops 2048 | bytes 16384 | tf_op jit(solution)/shard_map/psum | solution.py:54
  (8 shorter events, 0.1 us)
Async XLA Ops:
  7.2 66.4 %all-reduce.5.cloned.1.call-start = ((), (), s32[]{:S(2)}) async-start(), calls=%async_computation | async-start | bytes 131072 | tf_op jit(solution)/shard_map/psum | solution.py:24
  25.4 224.7 %all-reduce.7.cloned.1.call-start = ((), (), s32[]{:S(2)}) async-start(), calls=%async_computation.1 | async-start | bytes 131072 | tf_op jit(solution)/shard_map/psum | solution.py:25
  75.4 415.1 %all-reduce.9.cloned.1.call-start = ((), (), s32[]{:S(2)}) async-start(), calls=%async_computation.2 | async-start | bytes 16777216
  275.9 12.1 %copy-start = (f32[128,128]{1,0:T(8,128)}, f32[128,128]{1,0:T(8,128)S(1)}, u32[]{:S(2)}) copy-start(f32[128,128]{1,0:T(8,128)S(1)} %fusion.8) | copy-start | bytes 196612
  287.9 0.7 copy-start.4
  287.9 1.9 copy-start.2
  287.9 1.9 copy-start.3
  287.9 1.9 copy-start.1
Sparse Core Ops, SparseCore 0:
  25.5 48.0 all-reduce.4
  77.6 172.3 all-reduce.6
  288.1 202.3 all-reduce.8
where the time goes:
time: 508 us; the launch traced here: 507 us
  waiting for transfers between devices  423 us (83%)
  matrix products  32.3 us (6%)
  other arithmetic  25.3 us (5%)
  between operations  14.5 us (3%)
  blocking collectives  7.1 us (1%)
    unnamed x4, waiting for transfers between devices  201 us
    psum x1, waiting for transfers between devices, body(): lax.psum(jnp.dot(sketch.T, sketch, precision=highest, preferred_element_t...  174 us
    psum x1, waiting for transfers between devices, body(): sketch = lax.psum(partial_sketch, ('pa', 'pb'))  48.2 us
    dot_general x1, matrix products, body(): jnp.dot(flat, omega, precision=highest, preferred_element_type=jnp.float32)  16.7 us
    another operation x3, other arithmetic, body(): lower = jnp.linalg.cholesky(gram)  12.4 us
    dot_general x1, matrix products, body(): lax.dot_general(basis, flat, (((0,), (0,)), ((), ())), precision=highest,...  12.1 us
    another operation x2, other arithmetic, body(): lax.linalg.triangular_solve(lower, sketch, left_side=False, lower=True, t...  10.5 us
  transfers between devices with their start and end apart: 3, of which 3 were waited for; matrix products, arithmetic and copies ran while one was open for 0% of the time, Pallas kernels for 0%

commit v1 on v0

--- a/solution.py
+++ b/solution.py
@@ -21,7 +21,7 @@
         * g_fourth[None, None, None, :, :]
     ).reshape(width, RANK)
     partial_sketch = jnp.dot(flat, omega, precision=highest, preferred_element_type=jnp.float32)
-    sketch = lax.psum(partial_sketch, ("pa", "pb"))
+    sketch = lax.all_gather(partial_sketch, ("pa", "pb")).sum(axis=0)
     gram = lax.psum(
         jnp.dot(sketch.T, sketch, precision=highest, preferred_element_type=jnp.float32), "space"
     )

time: 508 us -> 470 us (0.925)
  waiting for transfers between devices: 423 us -> 373 us
  blocking collectives: 7.1 us -> 21.8 us
    psum x1 -> x0, waiting for transfers between devices: 48.2 us -> none  [body(): sketch = lax.psum(partial_sketch, ('pa', 'pb'))]
    all_gather x0 -> x1, blocking collectives: none -> 14.7 us  [body(): sketch = lax.all_gather(partial_sketch, ('pa', 'pb')).sum(axis=0)]
    unnamed x4 -> x3, waiting for transfers between devices: 201 us -> 200 us
  transfers between devices with their start and end apart: 3 -> 2, of which waited for: 3 -> 2; matrix products, arithmetic and copies ran while one was open for 0% -> 0% of each run, Pallas kernels for 0% -> 0%
where the time goes in v1:
time: 470 us
  waiting for transfers between devices  373 us (79%)
  matrix products  29.7 us (6%)
  other arithmetic  25.4 us (5%)
  blocking collectives  21.8 us (5%)
  between operations  14.8 us (3%)
  local copies, waits for them, and re-layouts  4.81 us (1%)
    unnamed x3, waiting for transfers between devices  200 us
    psum x1, waiting for transfers between devices, body(): lax.psum(jnp.dot(sketch.T, sketch, precision=highest, preferred_element_t...  173 us
    dot_general x1, matrix products, body(): jnp.dot(flat, omega, precision=highest, preferred_element_type=jnp.float32)  16.1 us
    all_gather x1, blocking collectives, body(): sketch = lax.all_gather(partial_sketch, ('pa', 'pb')).sum(axis=0)  14.7 us
    another operation x3, other arithmetic, body(): lower = jnp.linalg.cholesky(gram)  12.4 us
    dot_general x1, matrix products, body(): lax.dot_general(basis, flat, (((0,), (0,)), ((), ())), precision=highest,...  11.8 us
    another operation x2, other arithmetic, body(): lax.linalg.triangular_solve(lower, sketch, left_side=False, lower=True, t...  10.5 us
  transfers between devices with their start and end apart: 2, of which 2 were waited for; matrix products, arithmetic and copies ran while one was open for 0% of the time, Pallas kernels for 0%

profile of v1, /device:TPU:2, one launch (start us, length us, event | category | flops | bytes accessed | tf_op | source)
XLA Modules:
  0.0 469.8 jit_solution(6710109911577811992)
XLA Ops:
  7.2 0.0 all-reduce.4.cloned.1.call-start
  7.2 0.7 broadcast_multiply_fusion.3
  7.9 0.7 broadcast_multiply_fusion.1
  8.6 16.1 %fusion.4 = f32[128,128]{0,1:T(8,128)S(1)} fusion(f32[128,8,16,8,16]{0,4,3,2,1:T(8,128)} %param.8, f32[16,128]{1,0:T(8,128)} %param.12, f32[8,16,8,128]{3,2,1,0:T(8,128)S(1)} %broadcast_multiply_fusion.1), kind=kOutput, calls=%fused_computation.4 | convolution fusion | flops 3223322624 | bytes 8986624 | tf_op jit(solution)/shard_map/dot_general | solution.py:23
  24.8 14.7 %all-gather = f32[512,128]{0,1:T(8,128)S(1)} all-gather(f32[128,128]{0,1:T(8,128)S(1)} %fusion.4), channel_id=2, replica_groups=mesh['space'=64,'pa'=2,'pb'=2] {'pa','pb'}, dimensions={0}, use_global_device_ids=true | all-gather | bytes 327680 | tf_op jit(solution)/shard_map/all_gather | solution.py:24
  39.5 0.1 reshape.70
  39.6 0.2 reduce_sum.9
  39.7 0.9 fusion.11
  40.6 0.0 all-reduce.4.cloned.1.call-update
  40.6 0.2 all-reduce.6.cloned.1.call-start
  40.9 172.6 %all-reduce.4.cloned.1.call-done = f32[128,128]{0,1:T(8,128)} async-done(((f32[128,128]{0,1:T(8,128)}), f32[128,128]{0,1:T(8,128)}) %all-reduce.4.cloned.1.call-update) | async-done | bytes 65552 | tf_op jit(solution)/shard_map/psum | solution.py:25
  213.4 0.9 copy.14
  214.4 0.9 fusion.10
  215.2 11.7 %cholesky.16 = f32[128,128]{1,0:T(8,128)S(1)} custom-call(f32[128,128]{1,0:T(8,128)S(1)} %fusion.10), custom_call_target="Cholesky" | custom-call | tf_op jit(solution)/shard_map/jit(cholesky)/cholesky | solution.py:28
  227.0 0.6 compare_reduce_fusion
  227.6 0.7 fusion.7
  228.3 9.8 %custom-call.6 = f32[1,128,128]{1,2,0:T(8,128)S(1)} custom-call(f32[1,128,128]{2,1,0:T(8,128)S(1)} %fusion.7), custom_call_target="InvertDiagBlocksLowerTriangular" | custom-call | tf_op jit(solution)/shard_map/triangular_solve | solution.py:29
  238.1 0.3 fusion.8
  238.4 0.0 copy-start
  238.4 11.8 %fusion.12 = f32[128,16384]{1,0:T(8,128)} fusion(f32[128,128]{1,0:T(8,128)S(1)} %fusion.8, f32[128,16384]{0,1:T(8,128)} %bitcast.30), kind=kOutput, calls=%fused_computation.22 | convolution fusion | flops 3221225472 | bytes 16842752 | tf_op jit(solution)/shard_map/dot_general | solution.py:33
  250.2 0.0 copy-start.3
  250.2 0.0 copy-start.1
  250.2 0.0 all-reduce.6.cloned.1.call-update
  250.2 0.6 copy-done.4
  250.8 0.6 dynamic-slice
  252.1 0.1 broadcast_multiply_fusion
  252.2 200.5 %all-reduce.6.cloned.1.call-done = f32[128,16384]{1,0:T(8,128)} async-done(((f32[128,16384]{1,0:T(8,128)}), f32[128,16384]{1,0:T(8,128)}) %all-reduce.6.cloned.1.call-update) | async-done | bytes 8388624
  452.7 1.1 constant_dynamic-slice_fusion
  453.8 0.1 reshape.68
  453.9 1.4 reshape.67
  455.3 0.6 convolution_bitcast_fusion
  455.9 7.1 %psum.15 = f32[2,8,128]{2,1,0:T(8,128)} all-reduce(f32[2,8,128]{2,1,0:T(8,128)S(1)} %convolution_bitcast_fusion), channel_id=1, replica_groups=mesh['space'=64,'pa'=2,'pb'=2] {'pb'}, use_global_device_ids=true, to_apply=%region_5.6 | all-reduce | flops 2048 | bytes 16384 | tf_op jit(solution)/shard_map/psum | solution.py:54
  (8 shorter events, 0.1 us)
Async XLA Ops:
  7.2 206.3 %all-reduce.4.cloned.1.call-start = ((), (), s32[]{:S(2)}) async-start(), calls=%async_computation | async-start | bytes 131072 | tf_op jit(solution)/shard_map/psum | solution.py:25
  40.6 412.1 %all-reduce.6.cloned.1.call-start = ((), (), s32[]{:S(2)}) async-start(), calls=%async_computation.1 | async-start | bytes 16777216
  238.4 11.8 %copy-start = (f32[128,128]{1,0:T(8,128)}, f32[128,128]{1,0:T(8,128)S(1)}, u32[]{:S(2)}) copy-start(f32[128,128]{1,0:T(8,128)S(1)} %fusion.8) | copy-start | bytes 196612
  250.1 0.7 copy-start.4
  250.1 1.9 copy-start.2
  250.2 1.9 copy-start.3
  250.2 1.9 copy-start.1
Sparse Core Ops, SparseCore 0:
  40.8 172.6 all-reduce.3
  250.3 202.3 all-reduce.5
